TPU v7x, 256 devices: a whole 4x4x8 slice. The times are simulated.
256 devices in a mesh: row: 16 (over z, core), col: 16 (over y, x).
Axes of the slice: x: 4, y: 4, z: 8, core: 2. Of those that a mesh axis runs over, the one named last changes fastest.
Arguments:
- matrix: bfloat16 [4096, 262144], P('row', 'col'), may hold values from -60 to 60
- test_matrix: bfloat16 [262144, 512], P(('col', 'row')), may hold values from -0.0390625 to 0.0390625
Outputs:
- orthonormal: float32 [4096, 512], P(('row', 'col'))
- triangular: float32 [512, 512], replicated
All inputs are finite; a program needn't handle non-finite values.
Results may differ from a plain program's by a relative error of at most 0.0003.
Values may be sent and summed in bfloat16 or wider, within the bound.
No kernel may reach another device: no remote copies, remote signals or barrier semaphores. Data moves between devices by JAX's collectives and lax.ppermute only.
A program may use at most 128 MiB of HBM per device.

v0:
```python
import jax
import jax.numpy as jnp
from jax import lax
from jax.sharding import PartitionSpec as P


def probe_product(matrix, test_matrix):
    return jnp.dot(
        matrix,
        lax.all_gather(test_matrix, "row", axis=0, tiled=True),
        preferred_element_type=jnp.float32,
    )


def gram_term(own_rows):
    return jnp.dot(own_rows.T, own_rows, precision=lax.Precision.HIGHEST)


def shards(matrix, test_matrix):
    share_rows = matrix.shape[0] // lax.axis_size("col")
    total_rows = matrix.shape[0] * lax.axis_size("row")
    partial_value = probe_product(matrix, test_matrix)
    sketch = lax.psum(partial_value, "col")
    gram = lax.psum(gram_term(sketch), "row")
    own_rows = lax.dynamic_slice_in_dim(sketch, lax.axis_index("col") * share_rows, share_rows, 0)
    gram = gram / jnp.float32(total_rows)
    lower_factor = jnp.linalg.cholesky(gram)
    orthonormal = lax.linalg.triangular_solve(
        lower_factor, own_rows, left_side=False, lower=True, transpose_a=True
    )
    return (orthonormal, lower_factor.T)


def solution(mesh):
    in_specs = (P("row", "col"), P(("col", "row"), None))
    out_specs = (P(("row", "col"), None), P())
    return jax.shard_map(shards, mesh=mesh, in_specs=in_specs, out_specs=out_specs, check_vma=False)
```

profile of v0, /device:TPU:1, one launch (start us, length us, event | category | flops | bytes accessed | tf_op | source)
XLA Modules:
  0.0 478.8 jit_solution(10044351522613762331)
XLA Ops:
  7.9 101.4 %all-gather.2.cloned.1.call-done = bf16[16384,512]{1,0:T(8,128)(2,1)} async-done(((bf16[1024,512]{1,0:T(8,128)(2,1)}), bf16[16384,512]{1,0:T(8,128)(2,1)}) %all-gather.2.cloned.1.call-update) | async-done | bytes 16777232 | tf_op jit(solution)/shard_map/all_gather | solution.py:10
  109.4 13.4 %fusion.34 = f32[256,512]{1,0:T(8,128)} fusion(bf16[256,16384]{1,0:T(8,128)(2,1)} %param.2, bf16[16384,512]{1,0:T(8,128)(2,1)} %all-gather.2.cloned.1.call-done), kind=kOutput, calls=%fused_computation.71 | convolution fusion | flops 4294967296 | bytes 25690112 | tf_op jit(solution)/shard_map/dot_general | solution.py:8
  123.1 91.7 %all-reduce.4.cloned.1.call-done = f32[256,512]{1,0:T(8,128)} async-done(((f32[256,512]{1,0:T(8,128)}), f32[256,512]{1,0:T(8,128)}) %all-reduce.4.cloned.1.call-update) | async-done | bytes 524304 | tf_op jit(solution)/shard_map/psum | solution.py:23
  214.8 3.2 fusion.35
  218.1 113.7 %all-reduce.6.cloned.1.call-done = f32[512,512]{0,1:T(8,128)} async-done(((f32[512,512]{0,1:T(8,128)}), f32[512,512]{0,1:T(8,128)}) %all-reduce.6.cloned.1.call-update) | async-done | bytes 1048592 | tf_op jit(solution)/shard_map/psum | solution.py:24
  331.8 1.3 broadcast_multiply_fusion
  333.5 1.5 fusion
  334.9 11.7 %cholesky.104 = f32[128,128]{1,0:T(8,128)S(1)} custom-call(f32[128,128]{1,0:T(8,128)S(1)} %cholesky.266), custom_call_target="Cholesky" | custom-call | tf_op jit(solution)/shard_map/jit(cholesky)/cholesky | solution.py:27
  346.7 9.8 %custom-call.30 = f32[1,128,128]{1,2,0:T(8,128)S(1)} custom-call(f32[1,128,128]{2,1,0:T(8,128)S(1)} %get-tuple-element.33), custom_call_target="InvertDiagBlocksLowerTriangular" | custom-call | tf_op jit(solution)/shard_map/jit(cholesky)/cholesky | solution.py:27
  357.3 11.8 %cholesky.217 = f32[128,128]{1,0:T(8,128)S(1)} custom-call(f32[128,128]{1,0:T(8,128)S(1)} %cholesky.270), custom_call_target="Cholesky" | custom-call | tf_op jit(solution)/shard_map/jit(cholesky)/cholesky | solution.py:27
  369.2 9.8 %custom-call.31 = f32[1,128,128]{1,2,0:T(8,128)S(1)} custom-call(f32[1,128,128]{2,1,0:T(8,128)S(1)} %get-tuple-element.30), custom_call_target="InvertDiagBlocksLowerTriangular" | custom-call | tf_op jit(solution)/shard_map/jit(cholesky)/cholesky | solution.py:27
  379.7 11.7 %cholesky.238 = f32[128,128]{1,0:T(8,128)S(1)} custom-call(f32[128,128]{1,0:T(8,128)S(1)} %cholesky.275), custom_call_target="Cholesky" | custom-call | tf_op jit(solution)/shard_map/jit(cholesky)/cholesky | solution.py:27
  392.1 9.8 %custom-call.32 = f32[1,128,128]{1,2,0:T(8,128)S(1)} custom-call(f32[1,128,128]{2,1,0:T(8,128)S(1)} %get-tuple-element.27), custom_call_target="InvertDiagBlocksLowerTriangular" | custom-call | tf_op jit(solution)/shard_map/jit(cholesky)/cholesky | solution.py:27
  402.6 12.0 %cholesky.255 = f32[128,128]{1,0:T(8,128)S(1)} custom-call(f32[128,128]{1,0:T(8,128)S(1)} %convolution_subtract_fusion.2), custom_call_target="Cholesky" | custom-call | tf_op jit(solution)/shard_map/jit(cholesky)/cholesky | solution.py:27
  418.7 1.3 copy.6
  420.0 8.1 %while.1 = (s32[]{:T(128)}, f32[512,512]{1,0:T(8,128)S(1)}, s32[4,2]{0,1:T(2,128)S(1)}, f32[4,128,128]{2,1,0:T(8,128)S(1)}, s32[]{:T(128)}) while((s32[]{:T(128)}, f32[512,512]{1,0:T(8,128)S(1)}, s32[4,2]{0,1:T(2,128)S(1)}, f32[4,128,128]{2,1,0:T(8,128)S(1)}, s32[]{:T(128)}) %tuple.33), condition=%wide.while_cond, body=%wide.while_body.sunk | while | flops 2 | bytes 131181 | solution.py:28
  420.6 1.3 bitcast_dynamic-update-slice_fusion.2
  422.7 1.3 bitcast_dynamic-update-slice_fusion.2
  424.7 1.3 bitcast_dynamic-update-slice_fusion.2
  426.8 1.3 bitcast_dynamic-update-slice_fusion.2
  428.1 39.3 %custom-call.33 = f32[4,128,128]{1,2,0:T(8,128)S(1)} custom-call(f32[4,128,128]{2,1,0:T(8,128)S(1)} %get-tuple-element.9), custom_call_target="InvertDiagBlocksLowerTriangular" | custom-call | tf_op jit(solution)/shard_map/triangular_solve | solution.py:28
  468.3 0.9 convolution_subtract_fusion.5
  469.4 0.9 convolution_subtract_fusion.4
  470.5 1.0 convolution_subtract_fusion.3
  (41 shorter events, 10.5 us)
Async XLA Ops:
  7.2 102.2 %all-gather.2.cloned.1.call-start = ((), (), s32[]{:S(2)}) async-start(), calls=%async_computation | async-start | bytes 17825792 | tf_op jit(solution)/shard_map/all_gather | solution.py:10
  7.9 206.9 %all-reduce.4.cloned.1.call-start = ((), (), s32[]{:S(2)}) async-start(), calls=%async_computation.1 | async-start | bytes 1048576 | tf_op jit(solution)/shard_map/psum | solution.py:23
  122.8 209.0 %all-reduce.6.cloned.1.call-start = ((), (), s32[]{:S(2)}) async-start(), calls=%async_computation.2 | async-start | bytes 2097152 | tf_op jit(solution)/shard_map/psum | solution.py:24
Sparse Core Ops, SparseCore 0:
  9.8 99.5 all-gather.1
  123.0 91.8 all-reduce.3
  218.2 113.5 all-reduce.5
where the time goes:
time: 479 us
  waiting for transfers between devices  308 us (64%)
  other arithmetic  122 us (25%)
  matrix products  22.7 us (5%)
  between operations  16.5 us (3%)
  local copies, waits for them, and re-layouts  9.84 us (2%)
    psum x1, waiting for transfers between devices, shards(): gram = lax.psum(gram_term(sketch), 'row')  114 us
    all_gather x1, waiting for transfers between devices, probe_product(): lax.all_gather(test_matrix, 'row', axis=0, tiled=True)  101 us
    psum x1, waiting for transfers between devices, shards(): sketch = lax.psum(partial_value, 'col')  91.7 us
    another operation x14, other arithmetic, shards(): lower_factor = jnp.linalg.cholesky(gram)  78.8 us
    another operation x3, other arithmetic, shards(): lax.linalg.triangular_solve(lower_factor, own_rows, left_side=False, lowe...  40 us
    dot_general x1, matrix products, probe_product(): jnp.dot(matrix, lax.all_gather(test_matrix, 'row', axis=0, tiled=True), p...  13.4 us
  transfers between devices with their start and end apart: 3, of which 3 were waited for; matrix products, arithmetic and copies ran while one was open for 0% of the time, Pallas kernels for 0%

commit v1 on v0

--- a/solution.py
+++ b/solution.py
@@ -5,11 +5,41 @@
 
 
 def probe_product(matrix, test_matrix):
-    return jnp.dot(
-        matrix,
-        lax.all_gather(test_matrix, "row", axis=0, tiled=True),
-        preferred_element_type=jnp.float32,
-    )
+
+    def teams_edit(target):
+        res, side_arr, opened = (
+            jax.lax.axis_size("row"),
+            jax.lax.axis_index("row"),
+            target.shape[0],
+        )
+        row_out = lax.dynamic_update_slice_in_dim(
+            jnp.zeros(
+                [q * res if to_i == 0 else q for to_i, q in enumerate(target.shape)], target.dtype
+            ),
+            target,
+            side_arr * opened,
+            axis=0,
+        )
+        u1 = next_value = target
+        for b in tuple(range(1, res // 2 + 1)):
+            u1 = jax.lax.ppermute(
+                u1, axis_name="row", perm=[(to_i, (to_i + 1) % res) for to_i in range(res)]
+            )
+            row_out = lax.dynamic_update_slice_in_dim(
+                row_out, u1, (side_arr - b) % res * opened, axis=0
+            )
+            if 2 * b < res:
+                next_value = jax.lax.ppermute(
+                    next_value,
+                    axis_name="row",
+                    perm=[(to_i, (to_i - 1) % res) for to_i in range(res)],
+                )
+                row_out = lax.dynamic_update_slice_in_dim(
+                    row_out, next_value, (side_arr + b) % res * opened, axis=0
+                )
+        return row_out
+
+    return jnp.dot(matrix, teams_edit(test_matrix), preferred_element_type=jnp.float32)
 
 
 def gram_term(own_rows):

time: 479 us -> 512 us (1.069)
  starting transfers between devices: 0.3 us -> 46.4 us
  waiting for transfers between devices: 308 us -> 263 us
  local copies, waits for them, and re-layouts: 9.84 us -> 43.6 us
    all_gather x1 -> x0, waiting for transfers between devices: 101 us -> none  [probe_product(): lax.all_gather(test_matrix, 'row', axis=0, tiled=True)]
    ppermute x0 -> x15, waiting for transfers between devices: none -> 50.6 us  [the longest x8 48.1 us: teams_edit(): jax.lax.ppermute(u1, axis_name='row', perm=[(to_i, (to_i + 1) % res) for...]
    ppermute x0 -> x15, starting transfers between devices: none -> 46.2 us  [the longest x7 28.3 us: teams_edit(): jax.lax.ppermute(next_value, axis_name='row', perm=[(to_i, (to_i - 1) % r...]
    dynamic_update_slice x0 -> x16, local copies, waits for them, and re-layouts: none -> 22 us  [the longest x8 11 us: teams_edit(): lax.dynamic_update_slice_in_dim(row_out, u1, (side_arr - b) % res * opene...]
    broadcast_in_dim x0 -> x1, local copies, waits for them, and re-layouts: none -> 7.74 us  [teams_edit(): jnp.zeros([q * res if to_i == 0 else q for to_i, q in enumerate(target.sh...]
    psum x1, waiting for transfers between devices: 91.7 us -> 98.9 us  [shards(): sketch = lax.psum(partial_value, 'col')]
  transfers between devices with their start and end apart: 3 -> 17, of which waited for: 3 -> 13; matrix products, arithmetic and copies ran while one was open for 0% -> 6% of each run, Pallas kernels for 0% -> 0%
where the time goes in v1:
time: 512 us
  waiting for transfers between devices  263 us (51%)
  other arithmetic  123 us (24%)
  starting transfers between devices  46.4 us (9%)
  local copies, waits for them, and re-layouts  43.6 us (9%)
  matrix products  19 us (4%)
  between operations  16.8 us (3%)
    psum x1, waiting for transfers between devices, shards(): gram = lax.psum(gram_term(sketch), 'row')  114 us
    psum x1, waiting for transfers between devices, shards(): sketch = lax.psum(partial_value, 'col')  98.9 us
    another operation x14, other arithmetic, shards(): lower_factor = jnp.linalg.cholesky(gram)  78.8 us
    ppermute x8, waiting for transfers between devices, teams_edit(): jax.lax.ppermute(u1, axis_name='row', perm=[(to_i, (to_i + 1) % res) for...  48.1 us
    another operation x3, other arithmetic, shards(): lax.linalg.triangular_solve(lower_factor, own_rows, left_side=False, lowe...  40 us
    ppermute x7, starting transfers between devices, teams_edit(): jax.lax.ppermute(next_value, axis_name='row', perm=[(to_i, (to_i - 1) % r...  28.3 us
    ppermute x8, starting transfers between devices, teams_edit(): jax.lax.ppermute(u1, axis_name='row', perm=[(to_i, (to_i + 1) % res) for...  17.9 us
    another operation x12, local copies, waits for them, and re-layouts  11.1 us
  transfers between devices with their start and end apart: 17, of which 13 were waited for; matrix products, arithmetic and copies ran while one was open for 6% of the time, Pallas kernels for 0%

profile of v1, /device:TPU:1, one launch (start us, length us, event | category | flops | bytes accessed | tf_op | source)
XLA Modules:
  0.0 511.8 jit_solution(2066119512491011913)
XLA Ops:
  10.5 11.8 %collective-permute-done = bf16[1024,512]{1,0:T(8,128)(2,1)S(1)} collective-permute-done((bf16[1024,512]{1,0:T(8,128)(2,1)}, bf16[1024,512]{1,0:T(8,128)(2,1)S(1)}, u32[]{:S(2)}, u32[]{:S(2)}) %collective-permute-start) | collective-permute-done | bytes 1048608 | tf_op jit(solution)/shard_map/ppermute | solution.py:25
  26.7 9.7 %collective-permute-done.2 = bf16[1024,512]{1,0:T(8,128)(2,1)S(1)} collective-permute-done((bf16[1024,512]{1,0:T(8,128)(2,1)S(1)}, bf16[1024,512]{1,0:T(8,128)(2,1)S(1)}, u32[]{:S(2)}, u32[]{:S(2)}) %collective-permute-start.2) | collective-permute-done | bytes 1048608 | tf_op jit(solution)/shard_map/ppermute | solution.py:25
  42.2 8.5 %collective-permute-done.4 = bf16[1024,512]{1,0:T(8,128)(2,1)S(1)} collective-permute-done((bf16[1024,512]{1,0:T(8,128)(2,1)S(1)}, bf16[1024,512]{1,0:T(8,128)(2,1)S(1)}, u32[]{:S(2)}, u32[]{:S(2)}) %collective-permute-start.4) | collective-permute-done | bytes 1048608 | tf_op jit(solution)/shard_map/ppermute | solution.py:25
  54.0 3.6 collective-permute-start.7
  57.6 7.2 %collective-permute-done.6 = bf16[1024,512]{1,0:T(8,128)(2,1)S(1)} collective-permute-done((bf16[1024,512]{1,0:T(8,128)(2,1)S(1)}, bf16[1024,512]{1,0:T(8,128)(2,1)S(1)}, u32[]{:S(2)}, u32[]{:S(2)}) %collective-permute-start.6) | collective-permute-done | bytes 1048608 | tf_op jit(solution)/shard_map/ppermute | solution.py:25
  68.5 5.5 %collective-permute-start.9 = (bf16[1024,512]{1,0:T(8,128)(2,1)S(1)}, bf16[1024,512]{1,0:T(8,128)(2,1)}, u32[]{:S(2)}, u32[]{:S(2)}) collective-permute-start(bf16[1024,512]{1,0:T(8,128)(2,1)S(1)} %collective-permute-done.7), channel_id=1, source_target_pairs={{0,240},{16,0},{32,16},{48,32},{64,48},{80,64},{96,80},{112,96},{1... | collective-permute-start | bytes 3145736 | tf_op jit(solution)/shard_map/ppermute | solution.py:32
  74.0 6.1 %collective-permute-done.8 = bf16[1024,512]{1,0:T(8,128)(2,1)S(1)} collective-permute-done((bf16[1024,512]{1,0:T(8,128)(2,1)S(1)}, bf16[1024,512]{1,0:T(8,128)(2,1)S(1)}, u32[]{:S(2)}, u32[]{:S(2)}) %collective-permute-start.8) | collective-permute-done | bytes 1048608 | tf_op jit(solution)/shard_map/ppermute | solution.py:25
  83.1 6.4 %collective-permute-start.11 = (bf16[1024,512]{1,0:T(8,128)(2,1)}, bf16[1024,512]{1,0:T(8,128)(2,1)}, u32[]{:S(2)}, u32[]{:S(2)}) collective-permute-start(bf16[1024,512]{1,0:T(8,128)(2,1)} %collective-permute-done.9), channel_id=1, source_target_pairs={{0,240},{16,0},{32,16},{48,32},{64,48},{80,64},{96,80},{112,96},{1... | collective-permute-start | bytes 3145736 | tf_op jit(solution)/shard_map/ppermute | solution.py:32
  89.5 4.8 collective-permute-done.10
  96.9 7.7 %broadcast_in_dim.5 = bf16[16384,512]{1,0:T(8,128)(2,1)} broadcast(bf16[]{:T(256)} %constant.229.clone.1), dimensions={} | broadcast | bytes 16777218 | tf_op jit(solution)/shard_map/broadcast_in_dim | solution.py:16
  111.0 8.1 %collective-permute-start.13 = (bf16[1024,512]{1,0:T(8,128)(2,1)}, bf16[1024,512]{1,0:T(8,128)(2,1)S(1)}, u32[]{:S(2)}, u32[]{:S(2)}) collective-permute-start(bf16[1024,512]{1,0:T(8,128)(2,1)} %collective-permute-done.11), channel_id=1, source_target_pairs={{0,240},{16,0},{32,16},{48,32},{64,48},{80,64},{96,80},{112,96},{1... | collective-permute-start | bytes 3145736 | tf_op jit(solution)/shard_map/ppermute | solution.py:32
  134.8 9.1 %convolution_bitcast_fusion = f32[256,512]{0,1:T(8,128)} fusion(bf16[16384,512]{1,0:T(8,128)(2,1)} %constant_dynamic-update-slice_fusion.1, bf16[256,16384]{1,0:T(8,128)(2,1)S(1)} %bitcast.54), kind=kOutput, calls=%fused_computation.2 | convolution fusion | flops 4294967296 | bytes 25690112 | tf_op jit(solution)/shard_map/dot_general | solution.py:42
  144.2 98.9 %all-reduce.4.cloned.1.call-done = f32[256,512]{0,1:T(8,128)} async-done(((f32[256,512]{0,1:T(8,128)}), f32[256,512]{0,1:T(8,128)}) %all-reduce.4.cloned.1.call-update) | async-done | bytes 524304 | tf_op jit(solution)/shard_map/psum | solution.py:53
  243.1 3.3 fusion.37
  246.4 113.7 %all-reduce.6.cloned.1.call-done = f32[512,512]{0,1:T(8,128)} async-done(((f32[512,512]{0,1:T(8,128)}), f32[512,512]{0,1:T(8,128)}) %all-reduce.6.cloned.1.call-update) | async-done | bytes 1048592 | tf_op jit(solution)/shard_map/psum | solution.py:54
  363.3 11.7 %cholesky.104 = f32[128,128]{1,0:T(8,128)S(1)} custom-call(f32[128,128]{1,0:T(8,128)S(1)} %cholesky.266), custom_call_target="Cholesky" | custom-call | tf_op jit(solution)/shard_map/jit(cholesky)/cholesky | solution.py:57
  375.1 9.8 %custom-call.30 = f32[1,128,128]{1,2,0:T(8,128)S(1)} custom-call(f32[1,128,128]{2,1,0:T(8,128)S(1)} %get-tuple-element.33), custom_call_target="InvertDiagBlocksLowerTriangular" | custom-call | tf_op jit(solution)/shard_map/jit(cholesky)/cholesky | solution.py:57
  385.6 11.8 %cholesky.217 = f32[128,128]{1,0:T(8,128)S(1)} custom-call(f32[128,128]{1,0:T(8,128)S(1)} %cholesky.270), custom_call_target="Cholesky" | custom-call | tf_op jit(solution)/shard_map/jit(cholesky)/cholesky | solution.py:57
  397.5 9.8 %custom-call.31 = f32[1,128,128]{1,2,0:T(8,128)S(1)} custom-call(f32[1,128,128]{2,1,0:T(8,128)S(1)} %get-tuple-element.30), custom_call_target="InvertDiagBlocksLowerTriangular" | custom-call | tf_op jit(solution)/shard_map/jit(cholesky)/cholesky | solution.py:57
  408.0 11.7 %cholesky.238 = f32[128,128]{1,0:T(8,128)S(1)} custom-call(f32[128,128]{1,0:T(8,128)S(1)} %cholesky.275), custom_call_target="Cholesky" | custom-call | tf_op jit(solution)/shard_map/jit(cholesky)/cholesky | solution.py:57
  420.4 9.8 %custom-call.32 = f32[1,128,128]{1,2,0:T(8,128)S(1)} custom-call(f32[1,128,128]{2,1,0:T(8,128)S(1)} %get-tuple-element.27), custom_call_target="InvertDiagBlocksLowerTriangular" | custom-call | tf_op jit(solution)/shard_map/jit(cholesky)/cholesky | solution.py:57
  430.8 12.0 %cholesky.255 = f32[128,128]{1,0:T(8,128)S(1)} custom-call(f32[128,128]{1,0:T(8,128)S(1)} %convolution_subtract_fusion.2), custom_call_target="Cholesky" | custom-call | tf_op jit(solution)/shard_map/jit(cholesky)/cholesky | solution.py:57
  447.8 11.1 %while.1 = (s32[]{:T(128)}, f32[512,512]{1,0:T(8,128)}, s32[4,2]{0,1:T(2,128)S(1)}, f32[4,128,128]{2,1,0:T(8,128)S(1)}, s32[]{:T(128)}) while((s32[]{:T(128)}, f32[512,512]{1,0:T(8,128)}, s32[4,2]{0,1:T(2,128)S(1)}, f32[4,128,128]{2,1,0:T(8,128)S(1)}, s32[]{:T(128)}) %tuple.33), condition=%wide.while_cond, body=%wide.while_body.sunk | while | flops 2 | bytes 131181 | solution.py:58
  459.0 39.3 %custom-call.33 = f32[4,128,128]{1,2,0:T(8,128)S(1)} custom-call(f32[4,128,128]{2,1,0:T(8,128)S(1)} %get-tuple-element.9), custom_call_target="InvertDiagBlocksLowerTriangular" | custom-call | tf_op jit(solution)/shard_map/triangular_solve | solution.py:58
  (122 shorter events, 74.5 us)
Async XLA Ops:
  7.2 97.5 %copy-start.1 = (bf16[1024,512]{1,0:T(8,128)(2,1)S(1)}, bf16[1024,512]{1,0:T(8,128)(2,1)}, u32[]{:S(2)}) copy-start(bf16[1024,512]{1,0:T(8,128)(2,1)} %param.3) | copy-start | bytes 3145732
  7.2 235.9 %all-reduce.4.cloned.1.call-start = ((), (), s32[]{:S(2)}) async-start(), calls=%async_computation | async-start | bytes 1048576 | tf_op jit(solution)/shard_map/psum | solution.py:53
  7.2 15.1 %collective-permute-start = (bf16[1024,512]{1,0:T(8,128)(2,1)}, bf16[1024,512]{1,0:T(8,128)(2,1)S(1)}, u32[]{:S(2)}, u32[]{:S(2)}) collective-permute-start(bf16[1024,512]{1,0:T(8,128)(2,1)} %param.3), channel_id=1, source_target_pairs={{0,16},{16,32},{32,48},{48,64},{64,80},{80,96},{96,112},{112,128},... | collective-permute-start | bytes 3145736 | tf_op jit(solution)/shard_map/ppermute | solution.py:25
  10.2 14.7 %collective-permute-start.1 = (bf16[1024,512]{1,0:T(8,128)(2,1)}, bf16[1024,512]{1,0:T(8,128)(2,1)S(1)}, u32[]{:S(2)}, u32[]{:S(2)}) collective-permute-start(bf16[1024,512]{1,0:T(8,128)(2,1)} %param.3), channel_id=1, source_target_pairs={{0,240},{16,0},{32,16},{48,32},{64,48},{80,64},{96,80},{112,96},{1... | collective-permute-start | bytes 3145736 | tf_op jit(solution)/shard_map/ppermute | solution.py:32
  22.3 14.1 %collective-permute-start.2 = (bf16[1024,512]{1,0:T(8,128)(2,1)S(1)}, bf16[1024,512]{1,0:T(8,128)(2,1)S(1)}, u32[]{:S(2)}, u32[]{:S(2)}) collective-permute-start(bf16[1024,512]{1,0:T(8,128)(2,1)S(1)} %collective-permute-done), channel_id=1, source_target_pairs={{0,16},{16,32},{32,48},{48,64},{64,80},{80,96},{96,112},{112,128},... | collective-permute-start | bytes 3145736 | tf_op jit(solution)/shard_map/ppermute | solution.py:25
  25.0 14.5 %collective-permute-start.3 = (bf16[1024,512]{1,0:T(8,128)(2,1)S(1)}, bf16[1024,512]{1,0:T(8,128)(2,1)S(1)}, u32[]{:S(2)}, u32[]{:S(2)}) collective-permute-start(bf16[1024,512]{1,0:T(8,128)(2,1)S(1)} %collective-permute-done.1), channel_id=1, source_target_pairs={{0,240},{16,0},{32,16},{48,32},{64,48},{80,64},{96,80},{112,96},{1... | collective-permute-start | bytes 3145736 | tf_op jit(solution)/shard_map/ppermute | solution.py:32
  36.4 14.2 %collective-permute-start.4 = (bf16[1024,512]{1,0:T(8,128)(2,1)S(1)}, bf16[1024,512]{1,0:T(8,128)(2,1)S(1)}, u32[]{:S(2)}, u32[]{:S(2)}) collective-permute-start(bf16[1024,512]{1,0:T(8,128)(2,1)S(1)} %collective-permute-done.2), channel_id=1, source_target_pairs={{0,16},{16,32},{32,48},{48,64},{64,80},{80,96},{96,112},{112,128},... | collective-permute-start | bytes 3145736 | tf_op jit(solution)/shard_map/ppermute | solution.py:25
  39.5 14.5 %collective-permute-start.5 = (bf16[1024,512]{1,0:T(8,128)(2,1)S(1)}, bf16[1024,512]{1,0:T(8,128)(2,1)S(1)}, u32[]{:S(2)}, u32[]{:S(2)}) collective-permute-start(bf16[1024,512]{1,0:T(8,128)(2,1)S(1)} %collective-permute-done.3), channel_id=1, source_target_pairs={{0,240},{16,0},{32,16},{48,32},{64,48},{80,64},{96,80},{112,96},{1... | collective-permute-start | bytes 3145736 | tf_op jit(solution)/shard_map/ppermute | solution.py:32
  50.7 14.2 %collective-permute-start.6 = (bf16[1024,512]{1,0:T(8,128)(2,1)S(1)}, bf16[1024,512]{1,0:T(8,128)(2,1)S(1)}, u32[]{:S(2)}, u32[]{:S(2)}) collective-permute-start(bf16[1024,512]{1,0:T(8,128)(2,1)S(1)} %collective-permute-done.4), channel_id=1, source_target_pairs={{0,16},{16,32},{32,48},{48,64},{64,80},{80,96},{96,112},{112,128},... | collective-permute-start | bytes 3145736 | tf_op jit(solution)/shard_map/ppermute | solution.py:25
  54.0 29.0 %copy-start.8 = (bf16[1024,512]{1,0:T(8,128)(2,1)}, bf16[1024,512]{1,0:T(8,128)(2,1)S(1)}, u32[]{:S(2)}) copy-start(bf16[1024,512]{1,0:T(8,128)(2,1)S(1)} %collective-permute-done.5) | copy-start | bytes 3145732
  54.0 14.5 %collective-permute-start.7 = (bf16[1024,512]{1,0:T(8,128)(2,1)S(1)}, bf16[1024,512]{1,0:T(8,128)(2,1)S(1)}, u32[]{:S(2)}, u32[]{:S(2)}) collective-permute-start(bf16[1024,512]{1,0:T(8,128)(2,1)S(1)} %collective-permute-done.5), channel_id=1, source_target_pairs={{0,240},{16,0},{32,16},{48,32},{64,48},{80,64},{96,80},{112,96},{1... | collective-permute-start | bytes 3145736 | tf_op jit(solution)/shard_map/ppermute | solution.py:32
  65.9 14.2 %collective-permute-start.8 = (bf16[1024,512]{1,0:T(8,128)(2,1)S(1)}, bf16[1024,512]{1,0:T(8,128)(2,1)S(1)}, u32[]{:S(2)}, u32[]{:S(2)}) collective-permute-start(bf16[1024,512]{1,0:T(8,128)(2,1)S(1)} %collective-permute-done.6), channel_id=1, source_target_pairs={{0,16},{16,32},{32,48},{48,64},{64,80},{80,96},{96,112},{112,128},... | collective-permute-start | bytes 3145736 | tf_op jit(solution)/shard_map/ppermute | solution.py:25
  68.5 14.5 %collective-permute-start.9 = (bf16[1024,512]{1,0:T(8,128)(2,1)S(1)}, bf16[1024,512]{1,0:T(8,128)(2,1)}, u32[]{:S(2)}, u32[]{:S(2)}) collective-permute-start(bf16[1024,512]{1,0:T(8,128)(2,1)S(1)} %collective-permute-done.7), channel_id=1, source_target_pairs={{0,240},{16,0},{32,16},{48,32},{64,48},{80,64},{96,80},{112,96},{1... | collective-permute-start | bytes 3145736 | tf_op jit(solution)/shard_map/ppermute | solution.py:32
  80.1 14.2 %collective-permute-start.10 = (bf16[1024,512]{1,0:T(8,128)(2,1)S(1)}, bf16[1024,512]{1,0:T(8,128)(2,1)}, u32[]{:S(2)}, u32[]{:S(2)}) collective-permute-start(bf16[1024,512]{1,0:T(8,128)(2,1)S(1)} %collective-permute-done.8), channel_id=1, source_target_pairs={{0,16},{16,32},{32,48},{48,64},{64,80},{80,96},{96,112},{112,128},... | collective-permute-start | bytes 3145736 | tf_op jit(solution)/shard_map/ppermute | solution.py:25
  83.1 28.0 %collective-permute-start.11 = (bf16[1024,512]{1,0:T(8,128)(2,1)}, bf16[1024,512]{1,0:T(8,128)(2,1)}, u32[]{:S(2)}, u32[]{:S(2)}) collective-permute-start(bf16[1024,512]{1,0:T(8,128)(2,1)} %collective-permute-done.9), channel_id=1, source_target_pairs={{0,240},{16,0},{32,16},{48,32},{64,48},{80,64},{96,80},{112,96},{1... | collective-permute-start | bytes 3145736 | tf_op jit(solution)/shard_map/ppermute | solution.py:32
  94.3 25.9 %collective-permute-start.12 = (bf16[1024,512]{1,0:T(8,128)(2,1)}, bf16[1024,512]{1,0:T(8,128)(2,1)}, u32[]{:S(2)}, u32[]{:S(2)}) collective-permute-start(bf16[1024,512]{1,0:T(8,128)(2,1)} %collective-permute-done.10), channel_id=1, source_target_pairs={{0,16},{16,32},{32,48},{48,64},{64,80},{80,96},{96,112},{112,128},... | collective-permute-start | bytes 3145736 | tf_op jit(solution)/shard_map/ppermute | solution.py:25
  96.9 23.3 %copy-start.3 = (bf16[1024,512]{1,0:T(8,128)(2,1)S(1)}, bf16[1024,512]{1,0:T(8,128)(2,1)}, u32[]{:S(2)}) copy-start(bf16[1024,512]{1,0:T(8,128)(2,1)} %copy-done.2) | copy-start | bytes 3145732
  96.9 24.3 %copy-start.7 = (bf16[1024,512]{1,0:T(8,128)(2,1)S(1)}, bf16[1024,512]{1,0:T(8,128)(2,1)}, u32[]{:S(2)}) copy-start(bf16[1024,512]{1,0:T(8,128)(2,1)} %copy-done.6) | copy-start | bytes 3145732
  96.9 25.4 %copy-start.13 = (bf16[1024,512]{1,0:T(8,128)(2,1)S(1)}, bf16[1024,512]{1,0:T(8,128)(2,1)}, u32[]{:S(2)}) copy-start(bf16[1024,512]{1,0:T(8,128)(2,1)} %copy-done.12) | copy-start | bytes 3145732
  104.7 30.1 %slice-start = ((s8[8388608]{0:T(1024)(128)(4,1)}), s8[4194304]{0:T(1024)(128)(4,1)S(1)}, s32[]{:S(2)}) async-start(s8[8388608]{0:T(1024)(128)(4,1)} %bitcast.53), calls=%async_computation.2 | async-start | bytes 8388608
  111.0 21.6 %collective-permute-start.13 = (bf16[1024,512]{1,0:T(8,128)(2,1)}, bf16[1024,512]{1,0:T(8,128)(2,1)S(1)}, u32[]{:S(2)}, u32[]{:S(2)}) collective-permute-start(bf16[1024,512]{1,0:T(8,128)(2,1)} %collective-permute-done.11), channel_id=1, source_target_pairs={{0,240},{16,0},{32,16},{48,32},{64,48},{80,64},{96,80},{112,96},{1... | collective-permute-start | bytes 3145736 | tf_op jit(solution)/shard_map/ppermute | solution.py:32
  120.2 13.6 %collective-permute-start.14 = (bf16[1024,512]{1,0:T(8,128)(2,1)}, bf16[1024,512]{1,0:T(8,128)(2,1)S(1)}, u32[]{:S(2)}, u32[]{:S(2)}) collective-permute-start(bf16[1024,512]{1,0:T(8,128)(2,1)} %collective-permute-done.12), channel_id=1, source_target_pairs={{0,16},{16,32},{32,48},{48,64},{64,80},{80,96},{96,112},{112,128},... | collective-permute-start | bytes 3145736 | tf_op jit(solution)/shard_map/ppermute | solution.py:25
  144.0 216.2 %all-reduce.6.cloned.1.call-start = ((), (), s32[]{:S(2)}) async-start(), calls=%async_computation.1 | async-start | bytes 2097152 | tf_op jit(solution)/shard_map/psum | solution.py:54
  243.1 255.2 %copy-start = (f32[256,512]{0,1:T(8,128)S(1)}, f32[256,512]{0,1:T(8,128)}, u32[]{:S(2)}) copy-start(f32[256,512]{0,1:T(8,128)} %all-reduce.4.cloned.1.call-done) | copy-start | bytes 1572868
  (11 other events, 120.0 us)
Sparse Core Ops, SparseCore 0:
  144.1 98.9 all-reduce.3
  246.5 113.5 all-reduce.5
